TPU v7x, 256 devices: a whole 4x4x8 slice. The times are simulated.
256 devices in a mesh: gx: 32 (over y, z_hi, core), gz: 8 (over z_lo, x).
Axes of the slice: x: 4, y: 4, z: 8 (z_hi: 4, z_lo: 2; z = z_hi * 2 + z_lo), core: 2. Of those that a mesh axis runs over, the one named last changes fastest.
Arguments:
- scalars: float32 [2, 4096, 128, 256], P(None, 'gx', 'gz'), may hold values from -6 to 6
- diffusivity: float32 [4096, 128, 256], P('gx', 'gz'), may hold values from 0.01 to 0.1
- reaction_rate: float32 [4096, 128, 256], P('gx', 'gz'), may hold values from 0.05 to 1
- block_inverse: float32 [2, 32, 128, 128], P(None, 'gx'), may hold values from 0 to 1
- block_response: float32 [2, 32, 128], P(None, 'gx'), may hold values from 0 to 1, as said below
- mean_profile: float32 [2, 256], replicated, may hold values from -4 to 4
- recycle_gain: float32 [2, 256], replicated, may hold values from 0.5 to 1.5
- station_index: int32 [1], replicated, may hold values from 0 to 4095
- span_shift: int32 [1], replicated, may hold values from 0 to 127
Outputs:
- transported: float32 [2, 4096, 128, 256], P(None, 'gx', 'gz')
Inputs may be any that keep to these rules, and one draw needn't show every extreme that they name: `block_response`: every entry is positive.
All inputs are finite; a program needn't handle non-finite values.
Results may differ from a plain program's by a relative error of at most 0.0003.
Values sent between devices are 32-bit elements; how exact they have to be, the bound alone decides.
No kernel may reach another device: no remote copies, remote signals or barrier semaphores. Data moves between devices by JAX's collectives and lax.ppermute only.
A program may use at most 64 MiB of HBM per device.

v0:
```python
import jax
import jax.numpy as jnp
from jax import lax
from jax.sharding import PartitionSpec as P

reaction_yields = (-1.0, 1.0)


def from_root(x, axis, root):
    mine = lax.axis_index(axis) == root
    return lax.psum(jnp.where(mine, x, jnp.zeros_like(x)), axis)


def with_halo(x, sides, width, wrap):
    for axis, dim in sides:
        devices, length = (lax.axis_size(axis), x.shape[dim])
        up = [(i, (i + 1) % devices) for i in range(devices if wrap else devices - 1)]
        down = [(j, i) for i, j in up]
        last = lax.slice_in_dim(x, length - width, length, axis=dim)
        first = lax.slice_in_dim(x, 0, width, axis=dim)
        before = lax.ppermute(last, axis, up)
        after = lax.ppermute(first, axis, down)
        x = jnp.concatenate([before, x, after], axis=dim)
    return x


def prefix(part, axis, combine, identity):
    place = lax.axis_index(axis)
    gathered = jax.tree.map(lambda a: lax.all_gather(a, axis), part)
    state = jax.tree.map(lambda a, e: jnp.zeros_like(a) + jnp.asarray(e, a.dtype), part, identity)

    def one(hop, state):
        return combine(
            state, jax.tree.map(lambda a: lax.dynamic_index_in_dim(a, hop, 0, False), gathered)
        )

    return lax.fori_loop(0, place, one, state)


def fourth_order(padded, dimension, length):

    def shifted(offset):
        return lax.slice_in_dim(padded, offset, offset + length, axis=dimension)

    return (
        -shifted(0) + 16.0 * shifted(1) - 30.0 * shifted(2) + 16.0 * shifted(3) - shifted(4)
    ) / 12.0


def make_inflow(station_plane, mean_profile, recycle_gain, span_shift):
    span_mean = jnp.mean(station_plane, axis=1, keepdims=True)
    rolled = jnp.roll(station_plane, span_shift[0], axis=1)
    return mean_profile[:, None, :] + recycle_gain[:, None, :] * (rolled - span_mean)


def explicit_part(stream_padded, span_padded, center, diffusivity, reaction_rate):
    wall_padded = jnp.pad(center, ((0, 0), (0, 0), (0, 0), (2, 2)))
    laplacian = fourth_order(stream_padded, 1, center.shape[1])
    laplacian = laplacian + fourth_order(span_padded, 2, center.shape[2])
    laplacian = laplacian + fourth_order(wall_padded, 3, center.shape[3])
    reaction = reaction_rate * jax.nn.softplus(center[0]) * jax.nn.softplus(center[1])
    source = jnp.stack([reaction_yields[0] * reaction, reaction_yields[1] * reaction])
    return center + diffusivity[None] * laplacian + source


def on_device(
    scalars,
    diffusivity,
    reaction_rate,
    block_inverse,
    block_response,
    mean_profile,
    recycle_gain,
    station_index,
    span_shift,
):
    plane_count = scalars.shape[1]
    span_cells = scalars.shape[2]
    stream_devices = lax.axis_size("gx")
    stream_rank = lax.axis_index("gx")
    span_rank = lax.axis_index("gz")
    owner_row = station_index[0] // plane_count
    local_plane = station_index[0] - owner_row * plane_count
    own_slice = lax.dynamic_index_in_dim(scalars, local_plane, 1, keepdims=False)
    arrived = from_root(own_slice, "gx", owner_row)
    station_plane = lax.all_gather(arrived, "gz", axis=1, tiled=True)
    inflow_full = make_inflow(station_plane, mean_profile, recycle_gain, span_shift)
    inflow = lax.dynamic_slice_in_dim(inflow_full, span_rank * span_cells, span_cells, 1)
    stream_padded = with_halo(scalars, (("gx", 1),), 2, False)
    edge_shape = (scalars.shape[0], 2, scalars.shape[2], scalars.shape[3])
    inlet_planes = jnp.broadcast_to(inflow[:, None], edge_shape)
    outlet_planes = jnp.broadcast_to(scalars[:, -1:], edge_shape)
    head_planes = jnp.where(stream_rank == 0, inlet_planes, stream_padded[:, :2])
    tail_planes = jnp.where(stream_rank == stream_devices - 1, outlet_planes, stream_padded[:, -2:])
    window = jnp.concatenate([head_planes, stream_padded[:, 2:-2], tail_planes], axis=1)
    span_padded = with_halo(scalars, (("gz", 2),), 2, True)
    explicit = explicit_part(window, span_padded, scalars, diffusivity, reaction_rate)
    local_part = jnp.einsum(
        "sij,sjzy->sizy", block_inverse[:, 0], explicit, precision=lax.Precision.HIGHEST
    )
    response = block_response[:, 0]
    exit_plane = local_part[:, -1]
    exit_ratio = response[:, -1]

    def compose(earlier_part, later_part):
        return (
            earlier_part[0] * later_part[0],
            later_part[0][:, None, None] * earlier_part[1] + later_part[1],
        )

    identity = (jnp.ones_like(exit_ratio), jnp.zeros_like(exit_plane))
    through, upstream_sum = prefix((exit_ratio, exit_plane), "gx", compose, identity)
    incoming = through[:, None, None] * inflow + upstream_sum
    return local_part + response[:, :, None, None] * incoming[:, None]


def solution(mesh):
    return jax.shard_map(
        on_device,
        mesh=mesh,
        in_specs=(
            P(None, "gx", "gz", None),
            P("gx", "gz", None),
            P("gx", "gz", None),
            P(None, "gx", None, None),
            P(None, "gx", None),
            P(),
            P(),
            P(),
            P(),
        ),
        out_specs=P(None, "gx", "gz", None),
        check_vma=False,
    )
```

profile of v0, /device:TPU:217, one launch (start us, length us, event | category | flops | bytes accessed | tf_op | source)
XLA Modules:
  0.0 334.0 jit_solution(15417572126514026074)
XLA Ops:
  6.5 1.6 fusion.48
  8.1 1.3 collective-permute-start
  9.4 3.8 %collective-permute-start.1 = (f32[2,2,16,256]{3,2,1,0:T(8,128)}, f32[2,2,16,256]{3,2,1,0:T(8,128)}, u32[]{:S(2)}, u32[]{:S(2)}) collective-permute-start(f32[2,2,16,256]{3,2,1,0:T(8,128)} %get-tuple-element.62), channel_id=1, source_target_pairs={{8,0},{16,8},{24,16},{32,24},{40,32},{48,40},{56,48},{64,56},{72,6... | collective-permute-start | bytes 196616 | tf_op jit(solution)/shard_map/ppermute | solution.py:22
  13.3 3.6 %fusion.47 = (f32[2,128,2,256]{3,2,1,0:T(2,128)}, f32[2,128,2,256]{3,2,1,0:T(2,128)}) fusion(f32[2,128,16,256]{3,2,1,0:T(8,128)} %param.11), kind=kLoop, calls=%fused_computation.82 | loop fusion | bytes 2097152 | tf_op jit(solution)/shard_map/slice | solution.py:20
  16.9 2.9 collective-permute-start.3
  21.1 1.4 slice_bitcast_fusion
  22.5 0.9 slice_reduce_fusion
  24.2 1.3 dynamic-slice
  26.3 137.6 %all-reduce.2 = (f32[2,16,256]{2,1,0:T(8,128)S(1)}, f32[64]{0:T(128)S(1)}) all-reduce(f32[2,16,256]{2,1,0:T(8,128)S(1)} %fusion.44, f32[64]{0:T(128)S(1)} %dynamic-update-slice), channel_id=1, replica_groups=mesh['gx'=32,'gz'=8] {'gx'}, use_global_device_ids=true, to_apply=%region_0.1 | all-reduce | flops 8256 | bytes 66048 | tf_op jit(solution)/shard_map/psum | solution.py:11
  163.9 22.5 %all_gather.9 = f32[2,128,256]{2,1,0:T(8,128)S(1)} all-gather(f32[2,16,256]{2,1,0:T(8,128)S(1)} %get-tuple-element.53), channel_id=1, replica_groups=mesh['gx'=32,'gz'=8] {'gz'}, dimensions={1}, use_global_device_ids=true | all-gather | bytes 294912 | tf_op jit(solution)/shard_map/all_gather | solution.py:86
  186.5 6.7 %multiply_bitcast_fusion = (f32[1,128,16,256]{3,2,1,0:T(8,128)S(1)}, f32[128,16,256]{2,1,0:T(8,128)}) fusion(f32[2,128,16,256]{3,2,1,0:T(8,128)} %param.11, f32[128,16,256]{2,1,0:T(8,128)} %param.13), kind=kLoop, calls=%fused_computation.64 | loop fusion | flops 7864320 | bytes 10485760 | tf_op jit(solution)/shard_map/stack | solution.py:62
  193.1 1.6 broadcast_multiply_fusion
  195.4 4.7 %constant_dynamic-update-slice_fusion.1 = f32[2,128,18,256]{3,2,1,0:T(8,128)} fusion(f32[2,128,16,256]{3,2,1,0:T(8,128)} %param.11), kind=kLoop, calls=%fused_computation.78 | loop fusion | bytes 8388608
  200.0 0.9 broadcast_select_fusion.1
  201.7 1.1 constant_dynamic-update-slice_fusion
  202.7 25.1 %fusion.8 = f32[2,128,16,256]{3,2,1,0:T(8,128)S(1)} fusion(f32[2,128,16,256]{3,2,1,0:T(8,128)} %param.11, f32[2,2,16,256]{3,2,1,0:T(8,128)S(1)} %broadcast_select_fusion, f32[2,2,16,256]{3,2,1,0:T(8,128)S(1)} %broadcast_select_fusion.1, f32[2,128,2,256]{3,2,1,0:T(2,128)S(1)} %collective-permute-done.2, ...), kind=kLoop, calls=%fused_computation.22 | loop fusion | flops 35651584 | bytes 23724032 | tf_op jit(solution)/shard_map/add | solution.py:63
  227.8 6.3 %fusion.29 = f32[2,128,16,256]{3,1,2,0:T(8,128)S(1)} fusion(f32[2,128,16,256]{3,2,1,0:T(8,128)S(1)} %fusion.8, f32[2,1,128,128]{3,2,1,0:T(8,128)S(1)} %copy-done), kind=kOutput, calls=%fused_computation.49 | convolution fusion | flops 1610612736 | bytes 8519680 | tf_op jit(solution)/shard_map/sij,sjzy->sizy/dot_general | solution.py:98
  234.2 2.0 copy-done.1
  237.0 56.6 %all-gather.4.cloned.1.call-done = f32[64,1,16,256]{3,2,1,0:T(8,128)} async-done(((f32[2,1,16,256]{3,2,1,0:T(8,128)}), f32[64,1,16,256]{3,2,1,0:T(8,128)}) %all-gather.4.cloned.1.call-update) | async-done | bytes 1048592 | tf_op jit(solution)/shard_map/all_gather | solution.py:29
  293.6 26.3 %while.12 = (s32[]{:T(128)}, f32[2]{0:T(128)S(1)}, f32[2,16,256]{2,1,0:T(8,128)S(1)}, s32[]{:T(128)}, f32[32,2]{1,0:T(8,128)S(1)}, /*index=5*/f32[32,2,16,256]{3,2,1,0:T(8,128)}, s32[]{:T(128)}, s32[]{:T(128)}, s32[]{:T(128)}) while((s32[]{:T(128)}, f32[2]{0:T(128)S(1)}, f32[2,16,256]{2,1,0:T(8,128)S(1)}, s32[]{:T(128)}, ...), condition=%wide.region_3.4_spmd, body=%wide.region_2.3_spmd.sunk | while | flops 16391 | bytes 98479 | solution.py:37
  294.5 0.8 bitcast_add_fusion.2
  297.0 0.8 bitcast_add_fusion.2
  320.0 2.7 multiply_add_fusion
  322.7 4.4 %copy.19 = f32[2,128,16,256]{3,2,1,0:T(8,128)} copy(f32[2,128,16,256]{3,1,2,0:T(8,128)S(1)} %multiply_add_fusion) | data formatting | bytes 8388608 | tf_op jit(solution)/shard_map/add | solution.py:114
  (91 shorter events, 27.9 us)
Async XLA Ops:
  6.5 221.3 %copy-start = (f32[2,1,128,128]{3,2,1,0:T(8,128)S(1)}, f32[2,1,128,128]{3,2,1,0:T(8,128)}, u32[]{:S(2)}) copy-start(f32[2,1,128,128]{3,2,1,0:T(8,128)} %param.14) | copy-start | bytes 393220
  6.5 287.1 %all-gather.4.cloned.1.call-start = ((), (), s32[]{:S(2)}) async-start(), calls=%async_computation | async-start | bytes 1081344 | tf_op jit(solution)/shard_map/all_gather | solution.py:29
  8.1 191.9 %collective-permute-start = (f32[2,2,16,256]{3,2,1,0:T(8,128)}, f32[2,2,16,256]{3,2,1,0:T(8,128)}, u32[]{:S(2)}, u32[]{:S(2)}) collective-permute-start(f32[2,2,16,256]{3,2,1,0:T(8,128)} %get-tuple-element.61), channel_id=1, source_target_pairs={{0,8},{8,16},{16,24},{24,32},{32,40},{40,48},{48,56},{56,64},{64,7... | collective-permute-start | bytes 196616 | tf_op jit(solution)/shard_map/ppermute | solution.py:21
  9.4 191.5 %collective-permute-start.1 = (f32[2,2,16,256]{3,2,1,0:T(8,128)}, f32[2,2,16,256]{3,2,1,0:T(8,128)}, u32[]{:S(2)}, u32[]{:S(2)}) collective-permute-start(f32[2,2,16,256]{3,2,1,0:T(8,128)} %get-tuple-element.62), channel_id=1, source_target_pairs={{8,0},{16,8},{24,16},{32,24},{40,32},{48,40},{56,48},{64,56},{72,6... | collective-permute-start | bytes 196616 | tf_op jit(solution)/shard_map/ppermute | solution.py:22
  16.9 184.8 %collective-permute-start.3 = (f32[2,128,2,256]{3,2,1,0:T(2,128)}, f32[2,128,2,256]{3,2,1,0:T(2,128)S(1)}, u32[]{:S(2)}, u32[]{:S(2)}) collective-permute-start(f32[2,128,2,256]{3,2,1,0:T(2,128)} %get-tuple-element.59), channel_id=1, source_target_pairs={{1,0},{2,1},{3,2},{4,3},{5,4},{6,5},{7,6},{0,7},{9,8},{10,9},{11,1... | collective-permute-start | bytes 1572872 | tf_op jit(solution)/shard_map/ppermute | solution.py:22
  19.8 182.9 %collective-permute-start.2 = (f32[2,128,2,256]{3,2,1,0:T(2,128)}, f32[2,128,2,256]{3,2,1,0:T(2,128)S(1)}, u32[]{:S(2)}, u32[]{:S(2)}) collective-permute-start(f32[2,128,2,256]{3,2,1,0:T(2,128)} %get-tuple-element.60), channel_id=1, source_target_pairs={{0,1},{1,2},{2,3},{3,4},{4,5},{5,6},{6,7},{7,0},{8,9},{9,10},{10,1... | collective-permute-start | bytes 1572872 | tf_op jit(solution)/shard_map/ppermute | solution.py:21
  186.4 6.7 %copy-start.2 = (f32[128,16,256]{2,1,0:T(8,128)S(1)}, f32[128,16,256]{2,1,0:T(8,128)}, u32[]{:S(2)}) copy-start(f32[128,16,256]{2,1,0:T(8,128)} %param.12) | copy-start | bytes 6291460
  193.1 1.6 copy-start.3
  193.1 1.6 copy-start.4
  227.8 92.1 %copy-start.5 = (f32[2,1,128]{2,1,0:T(1,128)S(1)}, f32[2,1,128]{2,1,0:T(1,128)}, u32[]{:S(2)}) copy-start(f32[2,1,128]{2,1,0:T(1,128)} %param.15) | copy-start | bytes 3076
  234.2 2.0 copy-start.1
Sparse Core Ops, SparseCore 0:
  237.0 56.5 all-gather.3
where the time goes:
time: 337 us; the launch traced here: 334 us
  blocking collectives  160 us (47%)
  other arithmetic  65.5 us (19%)
  waiting for transfers between devices  56.6 us (17%)
  local copies, waits for them, and re-layouts  21.9 us (6%)
  between operations  15.5 us (5%)
  starting transfers between devices  8.06 us (2%)
  matrix products  6.35 us (2%)
    psum x1, blocking collectives, from_root(): return lax.psum(jnp.where(mine, x, jnp.zeros_like(x)), axis)  138 us
    all_gather x1, waiting for transfers between devices, prefix(): gathered = jax.tree.map(lambda a: lax.all_gather(a, axis), part)  56.6 us
    add x31, other arithmetic, compose(): later_part[0][:, None, None] * earlier_part[1] + later_part[1]  25.9 us
    add x1, other arithmetic, explicit_part(): return center + diffusivity[None] * laplacian + source  25.1 us
    all_gather x1, blocking collectives, on_device(): station_plane = lax.all_gather(arrived, 'gz', axis=1, tiled=True)  22.5 us
    unnamed x16, local copies, waits for them, and re-layouts  8.19 us
    ppermute x2, starting transfers between devices, with_halo(): after = lax.ppermute(first, axis, down)  6.77 us
  transfers between devices with their start and end apart: 5, of which 1 were waited for; matrix products, arithmetic and copies ran while one was open for 7% of the time, Pallas kernels for 0%

commit v1 on v0

--- a/solution.py
+++ b/solution.py
@@ -8,7 +8,7 @@
 
 def from_root(x, axis, root):
     mine = lax.axis_index(axis) == root
-    return lax.psum(jnp.where(mine, x, jnp.zeros_like(x)), axis)
+    return jnp.sum(lax.all_gather(jnp.where(mine, x, jnp.zeros_like(x)), axis), axis=0)
 
 
 def with_halo(x, sides, width, wrap):

time: 337 us -> 235 us (0.70)
  blocking collectives: 160 us -> 93.8 us
  waiting for transfers between devices: 56.6 us -> 24.6 us
  local copies, waits for them, and re-layouts: 21.9 us -> 18.2 us
    psum x1 -> x0, blocking collectives: 138 us -> none  [from_root(): return lax.psum(jnp.where(mine, x, jnp.zeros_like(x)), axis)]
    unnamed x0 -> x1, blocking collectives: none -> 71.3 us
    all_gather x1, waiting for transfers between devices: 56.6 us -> 0.02 us  [prefix(): gathered = jax.tree.map(lambda a: lax.all_gather(a, axis), part)]
    all_gather x0 -> x1, waiting for transfers between devices: none -> 24.5 us  [from_root(): lax.all_gather(jnp.where(mine, x, jnp.zeros_like(x)), axis)]
    unnamed x16 -> x20, local copies, waits for them, and re-layouts: 8.19 us -> 6.73 us
  transfers between devices with their start and end apart: 5 -> 6, of which waited for: 1 -> 1; matrix products, arithmetic and copies ran while one was open for 7% -> 9% of each run, Pallas kernels for 0% -> 0%
where the time goes in v1:
time: 235 us; the launch traced here: 233 us
  blocking collectives  93.8 us (40%)
  other arithmetic  66.5 us (28%)
  waiting for transfers between devices  24.6 us (10%)
  local copies, waits for them, and re-layouts  18.2 us (8%)
  between operations  15.6 us (7%)
  starting transfers between devices  7.47 us (3%)
  matrix products  6.35 us (3%)
    unnamed x1, blocking collectives  71.3 us
    add x31, other arithmetic, compose(): later_part[0][:, None, None] * earlier_part[1] + later_part[1]  25.9 us
    add x1, other arithmetic, explicit_part(): return center + diffusivity[None] * laplacian + source  24.9 us
    all_gather x1, waiting for transfers between devices, from_root(): lax.all_gather(jnp.where(mine, x, jnp.zeros_like(x)), axis)  24.5 us
    all_gather x1, blocking collectives, on_device(): station_plane = lax.all_gather(arrived, 'gz', axis=1, tiled=True)  22.5 us
    unnamed x20, local copies, waits for them, and re-layouts  6.73 us
    another operation x1, other arithmetic, explicit_part(): jnp.stack([reaction_yields[0] * reaction, reaction_yields[1] * reaction])  6.72 us
    dot_general x1, matrix products, on_device(): jnp.einsum('sij,sjzy->sizy', block_inverse[:, 0], explicit, precision=lax...  6.35 us
  transfers between devices with their start and end apart: 6, of which 1 were waited for; matrix products, arithmetic and copies ran while one was open for 9% of the time, Pallas kernels for 0%

profile of v1, /device:TPU:217, one launch (start us, length us, event | category | flops | bytes accessed | tf_op | source)
XLA Modules:
  0.0 232.6 jit_solution(1179631154448709611)
XLA Ops:
  7.3 1.4 dynamic-slice_select_fusion
  8.7 1.5 fusion.47
  10.2 1.3 collective-permute-start
  11.5 3.2 %collective-permute-start.1 = (f32[2,2,16,256]{3,2,1,0:T(8,128)S(1)}, f32[2,2,16,256]{3,2,1,0:T(8,128)S(1)}, u32[]{:S(2)}, u32[]{:S(2)}) collective-permute-start(f32[2,2,16,256]{3,2,1,0:T(8,128)S(1)} %get-tuple-element.62), channel_id=1, source_target_pairs={{8,0},{16,8},{24,16},{32,24},{40,32},{48,40},{56,48},{64,56},{72,6... | collective-permute-start | bytes 196616 | tf_op jit(solution)/shard_map/ppermute | solution.py:22
  14.8 3.6 %fusion.46 = (f32[2,128,2,256]{3,2,1,0:T(2,128)}, f32[2,128,2,256]{3,2,1,0:T(2,128)}) fusion(f32[2,128,16,256]{3,2,1,0:T(8,128)} %param.11), kind=kLoop, calls=%fused_computation.82 | loop fusion | bytes 2097152 | tf_op jit(solution)/shard_map/slice | solution.py:20
  18.3 2.9 %collective-permute-start.3 = (f32[2,128,2,256]{3,2,1,0:T(2,128)}, f32[2,128,2,256]{3,2,1,0:T(2,128)S(1)}, u32[]{:S(2)}, u32[]{:S(2)}) collective-permute-start(f32[2,128,2,256]{3,2,1,0:T(2,128)} %get-tuple-element.57), channel_id=1, source_target_pairs={{1,0},{2,1},{3,2},{4,3},{5,4},{6,5},{7,6},{0,7},{9,8},{10,9},{11,1... | collective-permute-start | bytes 1572872 | tf_op jit(solution)/shard_map/ppermute | solution.py:22
  21.2 6.7 %multiply_bitcast_fusion = (f32[1,128,16,256]{3,2,1,0:T(8,128)S(1)}, f32[128,16,256]{2,1,0:T(8,128)}) fusion(f32[2,128,16,256]{3,2,1,0:T(8,128)} %param.11, f32[128,16,256]{2,1,0:T(8,128)} %param.13), kind=kLoop, calls=%fused_computation.64 | loop fusion | flops 7864320 | bytes 10485760 | tf_op jit(solution)/shard_map/stack | solution.py:62
  28.0 1.6 broadcast_multiply_fusion
  29.6 1.4 copy-done.1
  30.9 2.5 %constant_dynamic-update-slice_fusion.1 = f32[2,128,18,256]{3,2,1,0:T(8,128)} fusion(f32[2,128,16,256]{3,2,1,0:T(8,128)S(1)} %copy-done.1), kind=kLoop, calls=%fused_computation.78 | loop fusion | bytes 8388608
  34.7 1.0 constant_dynamic-update-slice_fusion
  35.7 24.5 %all-gather.6.cloned.1.call-done = f32[64,1,16,256]{3,2,1,0:T(8,128)} async-done(((f32[2,1,16,256]{3,2,1,0:T(8,128)}), f32[64,1,16,256]{3,2,1,0:T(8,128)}) %all-gather.6.cloned.1.call-update) | async-done | bytes 1048592 | tf_op jit(solution)/shard_map/all_gather | solution.py:11
  60.3 1.3 bitcast_reduce_fusion
  61.5 22.5 %all_gather.14 = f32[2,128,256]{2,1,0:T(8,128)S(1)} all-gather(f32[2,16,256]{2,1,0:T(8,128)S(1)} %bitcast_reduce_fusion), channel_id=1, replica_groups=mesh['gx'=32,'gz'=8] {'gz'}, dimensions={1}, use_global_device_ids=true | all-gather | bytes 294912 | tf_op jit(solution)/shard_map/all_gather | solution.py:86
  84.2 0.9 broadcast_select_fusion.1
  85.1 24.9 %fusion.8 = f32[2,128,16,256]{3,2,1,0:T(8,128)S(1)} fusion(f32[2,128,16,256]{3,2,1,0:T(8,128)} %param.11, f32[2,2,16,256]{3,2,1,0:T(8,128)} %broadcast_select_fusion, f32[2,2,16,256]{3,2,1,0:T(8,128)S(1)} %broadcast_select_fusion.1, f32[2,128,2,256]{3,2,1,0:T(2,128)S(1)} %collective-permute-done.2, f32[2,128,18,256]{3,2,1,0:T(8,128)} %constant_dynamic-update-slice_fusion, ...), kind=kLoop, calls=%fused_computation.22 | loop fusion | flops 35651584 | bytes 23724032 | tf_op jit(solution)/shard_map/add | solution.py:63
  110.0 6.3 %fusion.29 = f32[2,128,16,256]{3,1,2,0:T(8,128)S(1)} fusion(f32[2,128,16,256]{3,2,1,0:T(8,128)S(1)} %fusion.8, f32[2,1,128,128]{3,2,1,0:T(8,128)S(1)} %copy-done), kind=kOutput, calls=%fused_computation.49 | convolution fusion | flops 1610612736 | bytes 8519680 | tf_op jit(solution)/shard_map/sij,sjzy->sizy/dot_general | solution.py:98
  116.3 2.0 copy-done.2
  120.7 71.3 %all-reduce.1 = f32[64]{0:T(128)S(1)} all-reduce(f32[64]{0:T(128)S(1)} %dynamic-update-slice), channel_id=3, replica_groups=mesh['gx'=32,'gz'=8] {'gx'}, use_global_device_ids=true, to_apply=%add.1 | all-reduce | flops 64 | bytes 512
  192.2 26.3 %while.12 = (s32[]{:T(128)}, f32[2]{0:T(128)S(1)}, f32[2,16,256]{2,1,0:T(8,128)S(1)}, s32[]{:T(128)}, f32[32,2]{1,0:T(8,128)S(1)}, /*index=5*/f32[32,2,16,256]{3,2,1,0:T(8,128)}, s32[]{:T(128)}, s32[]{:T(128)}, s32[]{:T(128)}) while((s32[]{:T(128)}, f32[2]{0:T(128)S(1)}, f32[2,16,256]{2,1,0:T(8,128)S(1)}, s32[]{:T(128)}, ...), condition=%wide.region_3.4_spmd, body=%wide.region_2.3_spmd.sunk | while | flops 16391 | bytes 98479 | solution.py:37
  192.3 0.8 bitcast_add_fusion.2
  194.8 0.8 bitcast_add_fusion.2
  218.6 2.7 %multiply_add_fusion = f32[2,128,16,256]{3,1,2,0:T(8,128)S(1)} fusion(f32[2,128,16,256]{3,1,2,0:T(8,128)} %copy-done.2, f32[2,16,256]{2,1,0:T(8,128)S(1)} %multiply_add_fusion.1, f32[2,128]{1,0:T(2,128)S(1)} %bitcast.74), kind=kLoop, calls=%fused_computation.48 | loop fusion | flops 2097152 | bytes 8422400 | tf_op jit(solution)/shard_map/add | solution.py:114
  221.4 4.4 %copy.16 = f32[2,128,16,256]{3,2,1,0:T(8,128)} copy(f32[2,128,16,256]{3,1,2,0:T(8,128)S(1)} %multiply_add_fusion) | data formatting | bytes 8388608 | tf_op jit(solution)/shard_map/add | solution.py:114
  (98 shorter events, 27.3 us)
Async XLA Ops:
  6.5 103.4 %copy-start = (f32[2,1,128,128]{3,2,1,0:T(8,128)S(1)}, f32[2,1,128,128]{3,2,1,0:T(8,128)}, u32[]{:S(2)}) copy-start(f32[2,1,128,128]{3,2,1,0:T(8,128)} %param.14) | copy-start | bytes 393220
  6.5 53.7 %all-gather.6.cloned.1.call-start = ((), (), s32[]{:S(2)}) async-start(), calls=%async_computation | async-start | bytes 1081344 | tf_op jit(solution)/shard_map/all_gather | solution.py:11
  8.7 183.5 %all-gather.8.cloned.1.call-start = ((), (), s32[]{:S(2)}) async-start(), calls=%async_computation.1 | async-start | bytes 1081344 | tf_op jit(solution)/shard_map/all_gather | solution.py:29
  10.2 73.9 %collective-permute-start = (f32[2,2,16,256]{3,2,1,0:T(8,128)}, f32[2,2,16,256]{3,2,1,0:T(8,128)}, u32[]{:S(2)}, u32[]{:S(2)}) collective-permute-start(f32[2,2,16,256]{3,2,1,0:T(8,128)} %get-tuple-element.61), channel_id=1, source_target_pairs={{0,8},{8,16},{16,24},{24,32},{32,40},{40,48},{48,56},{56,64},{64,7... | collective-permute-start | bytes 196616 | tf_op jit(solution)/shard_map/ppermute | solution.py:21
  11.5 22.5 %collective-permute-start.1 = (f32[2,2,16,256]{3,2,1,0:T(8,128)S(1)}, f32[2,2,16,256]{3,2,1,0:T(8,128)S(1)}, u32[]{:S(2)}, u32[]{:S(2)}) collective-permute-start(f32[2,2,16,256]{3,2,1,0:T(8,128)S(1)} %get-tuple-element.62), channel_id=1, source_target_pairs={{8,0},{16,8},{24,16},{32,24},{40,32},{48,40},{56,48},{64,56},{72,6... | collective-permute-start | bytes 196616 | tf_op jit(solution)/shard_map/ppermute | solution.py:22
  18.3 16.4 %collective-permute-start.3 = (f32[2,128,2,256]{3,2,1,0:T(2,128)}, f32[2,128,2,256]{3,2,1,0:T(2,128)S(1)}, u32[]{:S(2)}, u32[]{:S(2)}) collective-permute-start(f32[2,128,2,256]{3,2,1,0:T(2,128)} %get-tuple-element.57), channel_id=1, source_target_pairs={{1,0},{2,1},{3,2},{4,3},{5,4},{6,5},{7,6},{0,7},{9,8},{10,9},{11,1... | collective-permute-start | bytes 1572872 | tf_op jit(solution)/shard_map/ppermute | solution.py:22
  21.2 6.7 %copy-start.3 = (f32[128,16,256]{2,1,0:T(8,128)S(1)}, f32[128,16,256]{2,1,0:T(8,128)}, u32[]{:S(2)}) copy-start(f32[128,16,256]{2,1,0:T(8,128)} %param.12) | copy-start | bytes 6291460
  21.2 63.8 %collective-permute-start.2 = (f32[2,128,2,256]{3,2,1,0:T(2,128)}, f32[2,128,2,256]{3,2,1,0:T(2,128)S(1)}, u32[]{:S(2)}, u32[]{:S(2)}) collective-permute-start(f32[2,128,2,256]{3,2,1,0:T(2,128)} %get-tuple-element.58), channel_id=1, source_target_pairs={{0,1},{1,2},{2,3},{3,4},{4,5},{5,6},{6,7},{7,0},{8,9},{9,10},{10,1... | collective-permute-start | bytes 1572872 | tf_op jit(solution)/shard_map/ppermute | solution.py:21
  28.0 3.0 %copy-start.1 = (f32[2,128,16,256]{3,2,1,0:T(8,128)S(1)}, f32[2,128,16,256]{3,2,1,0:T(8,128)}, u32[]{:S(2)}) copy-start(f32[2,128,16,256]{3,2,1,0:T(8,128)} %param.11) | copy-start | bytes 12582916
  30.9 53.2 %copy-start.4 = (f32[2,256]{1,0:T(2,128)S(1)}, f32[2,256]{1,0:T(2,128)}, u32[]{:S(2)}) copy-start(f32[2,256]{1,0:T(2,128)} %param.16) | copy-start | bytes 6148
  30.9 53.2 %copy-start.5 = (f32[2,256]{1,0:T(2,128)S(1)}, f32[2,256]{1,0:T(2,128)}, u32[]{:S(2)}) copy-start(f32[2,256]{1,0:T(2,128)} %param.17) | copy-start | bytes 6148
  110.0 9.1 %copy-start.7 = (u32[256]{0:T(256)S(1)}, u32[256]{0:T(256)}, u32[]{:S(2)}) copy-start(u32[256]{0:T(256)} %constant.95) | copy-start | bytes 3076
  110.0 10.3 %copy-start.6 = (f32[2,1,128]{2,1,0:T(1,128)S(1)}, f32[2,1,128]{2,1,0:T(1,128)}, u32[]{:S(2)}) copy-start(f32[2,1,128]{2,1,0:T(1,128)} %param.15) | copy-start | bytes 3076
  116.3 2.0 copy-start.2
Sparse Core Ops, SparseCore 0:
  9.9 50.2 all-gather.5
  119.1 55.4 all-gather.7
